TPU v7x, 128 devices: a whole 4x4x4 slice. The times are simulated.
128 devices in a mesh: grp: 16 (over y, z), lag: 8 (over x, core).
Axes of the slice: x: 4, y: 4, z: 4, core: 2. Of those that a mesh axis runs over, the one named last changes fastest.
Arguments:
- history: float32 [16, 512, 32, 128], P('lag', 'grp'), may hold values from -6 to 6
- tiles: bfloat16 [65536, 128, 128], P(('grp', 'lag')), may hold values from -0.01171875 to 0.01171875
- tile_src: int32 [65536], P(('grp', 'lag')), may hold values from 0 to 511
- tile_obs: int32 [65536], P(('grp', 'lag')), may hold values from 0 to 32
- tile_lag: int32 [65536], P(('grp', 'lag')), may hold values from 0 to 1
- incident: float32 [32, 32, 128], P('grp', 'lag'), may hold values from -6 to 6
- near_inverse: bfloat16 [32, 128, 128], P('grp'), may hold values from -0.5 to 0.5
Outputs:
- field: float32 [32, 32, 128], P('grp', 'lag')
- new_current: float32 [32, 32, 128], P('grp', 'lag')
Inputs may be any that keep to these rules, and one draw needn't show every extreme that they name: `tile_obs`: a value of 32 marks a padded tile.
All inputs are finite; a program needn't handle non-finite values.
Results may differ from a plain program's by a relative error of at most 0.0035.
Values may be sent and summed in bfloat16 or wider, within the bound.
No kernel may reach another device: no remote copies, remote signals or barrier semaphores. Data moves between devices by JAX's collectives and lax.ppermute only.
A program may use at most 128 MiB of HBM per device.

v0:
```python
import jax
import jax.numpy as jnp
from jax import lax
from jax.sharding import PartitionSpec as P

OBS_DEV = 2


def body(history, tiles, tile_src, tile_obs, tile_lag, incident, near_inverse):
    hist16 = history.astype(jnp.bfloat16)
    gathered = lax.all_gather(hist16, "grp", axis=1, tiled=True)
    lag_count = gathered.shape[0]
    source_count = gathered.shape[1]
    flat = gathered.reshape(lag_count * source_count, gathered.shape[2], gathered.shape[3])
    picked = flat[tile_lag * source_count + tile_src]
    terms = jnp.einsum("kas,kos->kao", picked, tiles, preferred_element_type=jnp.float32)
    observers = OBS_DEV * lax.axis_size("grp")
    partial_field = jax.ops.segment_sum(terms, tile_obs, num_segments=observers)
    angle_part = incident.shape[1]
    summed = lax.psum(partial_field, "lag")
    mine = lax.psum_scatter(summed, "grp", scatter_dimension=0, tiled=True)
    field = lax.dynamic_slice_in_dim(mine, lax.axis_index("lag") * angle_part, angle_part, 1)
    rhs = (incident - field).astype(jnp.bfloat16)
    new_current = jnp.einsum("oag,ohg->oah", rhs, near_inverse, preferred_element_type=jnp.float32)
    return (field, new_current)


def solution(mesh):
    return jax.shard_map(
        body,
        mesh=mesh,
        in_specs=(
            P("lag", "grp", None, None),
            P(("grp", "lag"), None, None),
            P(("grp", "lag")),
            P(("grp", "lag")),
            P(("grp", "lag")),
            P("grp", "lag", None),
            P("grp", None, None),
        ),
        out_specs=(P("grp", "lag", None), P("grp", "lag", None)),
        check_vma=False,
    )
```

profile of v0, /device:TPU:0, one launch (start us, length us, event | category | flops | bytes accessed | tf_op | source)
XLA Modules:
  0.0 255.2 jit_solution(2422170448194656881)
XLA Ops:
  7.2 0.0 copy-start
  7.2 0.0 all-gather.2.cloned.1.call-start
  7.2 2.2 convert_element_type.6
  9.4 0.0 all-gather.2.cloned.1.call-update
  9.4 0.0 reduce-scatter.2.cloned.1.call-start
  9.5 0.7 compare_select_fusion
  10.2 73.4 %all-gather.2.cloned.1.call-done = bf16[2,512,32,128]{3,2,1,0:T(8,128)(2,1)} async-done(((bf16[2,32,32,128]{3,2,1,0:T(8,128)(2,1)}), bf16[2,512,32,128]{3,2,1,0:T(8,128)(2,1)}) %all-gather.2.cloned.1.call-update) | async-done | bytes 8388624 | tf_op jit(solution)/shard_map/all_gather | solution.py:11
  83.6 6.5 %gather_fusion = bf16[512,32,128]{2,1,0:T(8,128)(2,1)} fusion(bf16[1024,32,128]{2,1,0:T(8,128)(2,1)} %bitcast.4, s32[1024]{0:T(1024)S(1)} %pad_clamp_fusion), kind=kCustom, calls=%fused_computation | custom fusion | bytes 8390656 | tf_op jit(solution)/shard_map/gather | solution.py:15
  90.1 0.0 copy-start.4
  90.1 15.0 %fusion.1 = f32[512,32,128]{2,1,0:T(8,128)} fusion(bf16[512,32,128]{2,1,0:T(8,128)(2,1)} %gather_fusion, bf16[512,128,128]{2,1,0:T(8,128)(2,1)} %param.8), kind=kOutput, calls=%fused_computation.7 | convolution fusion | flops 536870912 | bytes 29360128 | tf_op jit(solution)/shard_map/kas,kos->kao/dot_general | solution.py:16
  105.2 0.0 copy-done.4
  105.2 0.0 copy-start.3
  105.2 44.7 %scatter_fusion = f32[32,32,128]{2,1,0:T(8,128)S(1)} fusion(f32[32,32,128]{2,1,0:T(8,128)S(1)} %broadcast_in_dim.9, s32[512]{0:T(512)S(1)} %copy-done.4, f32[512,32,128]{2,1,0:T(8,128)} %fusion.1), kind=kCustom, calls=%fused_computation.1 | custom fusion | flops 2097152 | bytes 25167872 | tf_op jit(solution)/shard_map/scatter-add | solution.py:18
  149.9 0.0 copy-start.1
  149.9 0.8 copy-done.1
  150.7 0.0 reduce-scatter.2.cloned.1.call-update
  150.7 72.3 %reduce-scatter.2.cloned.1.call-done = f32[2,32,128]{2,1,0:T(8,128)} async-done(((f32[32,32,128]{2,1,0:T(8,128)}), f32[2,32,128]{2,1,0:T(8,128)}) %reduce-scatter.2.cloned.1.call-update) | async-done | bytes 32784 | tf_op jit(solution)/shard_map/reduce_scatter | solution.py:21
  223.0 24.6 %psum.8 = f32[2,32,128]{2,1,0:T(8,128)S(1)} all-reduce(f32[2,32,128]{2,1,0:T(8,128)} %reduce-scatter.2.cloned.1.call-done), channel_id=1, replica_groups=mesh['grp'=16,'lag'=8] {'lag'}, use_global_device_ids=true, to_apply=%region_1.0 | all-reduce | flops 8192 | bytes 65536 | tf_op jit(solution)/shard_map/psum | solution.py:20
  247.6 0.0 copy-done
  247.6 0.0 copy-done.3
  247.6 0.0 copy-start.2
  247.6 0.7 fusion
  248.4 0.0 copy-done.2
  (3 shorter events, 0.1 us)
Async XLA Ops:
  7.2 240.4 %copy-start = (bf16[2,128,128]{2,1,0:T(8,128)(2,1)S(1)}, bf16[2,128,128]{2,1,0:T(8,128)(2,1)}, u32[]{:S(2)}) copy-start(bf16[2,128,128]{2,1,0:T(8,128)(2,1)} %param.13) | copy-start | bytes 196612
  7.2 76.4 %all-gather.2.cloned.1.call-start = ((), (), s32[]{:S(2)}) async-start(), calls=%async_computation.1 | async-start | bytes 8912896 | tf_op jit(solution)/shard_map/all_gather | solution.py:11
  9.4 213.6 %reduce-scatter.2.cloned.1.call-start = ((), (), s32[]{:S(2)}) async-start(), calls=%async_computation.2 | async-start | bytes 557056 | tf_op jit(solution)/shard_map/reduce_scatter | solution.py:21
  90.1 15.0 %copy-start.4 = (s32[512]{0:T(512)S(1)}, s32[512]{0:T(512)}, u32[]{:S(2)}) copy-start(s32[512]{0:T(512)} %param.10) | copy-start | bytes 6148
  105.2 142.4 %copy-start.3 = (f32[2,4,128]{2,1,0:T(4,128)S(1)}, f32[2,4,128]{2,1,0:T(4,128)}, u32[]{:S(2)}) copy-start(f32[2,4,128]{2,1,0:T(4,128)} %param.12) | copy-start | bytes 12292
  149.9 0.8 copy-start.1
  247.6 0.8 copy-start.2
Sparse Core Ops, SparseCore 0:
  10.2 73.3 all-gather.1
  150.8 72.1 reduce-scatter.1
where the time goes:
time: 256 us; the launch traced here: 255 us
  waiting for transfers between devices  146 us (57%)
  other arithmetic  47.6 us (19%)
  blocking collectives  24.6 us (10%)
  matrix products  15.7 us (6%)
  between operations  14.1 us (6%)
  local copies, waits for them, and re-layouts  7.41 us (3%)
    all_gather x1, waiting for transfers between devices, body(): gathered = lax.all_gather(hist16, 'grp', axis=1, tiled=True)  73.4 us
    reduce_scatter x1, waiting for transfers between devices, body(): mine = lax.psum_scatter(summed, 'grp', scatter_dimension=0, tiled=True)  72.3 us
    scatter-add x1, other arithmetic, body(): partial_field = jax.ops.segment_sum(terms, tile_obs, num_segments=observers)  44.7 us
    psum x1, blocking collectives, body(): summed = lax.psum(partial_field, 'lag')  24.6 us
    dot_general x1, matrix products, body(): jnp.einsum('kas,kos->kao', picked, tiles, preferred_element_type=jnp.floa...  15 us
    gather x1, local copies, waits for them, and re-layouts, body(): picked = flat[tile_lag * source_count + tile_src]  6.55 us
  transfers between devices with their start and end apart: 2, of which 2 were waited for; matrix products, arithmetic and copies ran while one was open for 0% of the time, Pallas kernels for 0%

commit v1 on v0

--- a/solution.py
+++ b/solution.py
@@ -17,7 +17,7 @@
     observers = OBS_DEV * lax.axis_size("grp")
     partial_field = jax.ops.segment_sum(terms, tile_obs, num_segments=observers)
     angle_part = incident.shape[1]
-    summed = lax.psum(partial_field, "lag")
+    summed = jnp.sum(lax.all_gather(partial_field, "lag"), axis=0)
     mine = lax.psum_scatter(summed, "grp", scatter_dimension=0, tiled=True)
     field = lax.dynamic_slice_in_dim(mine, lax.axis_index("lag") * angle_part, angle_part, 1)
     rhs = (incident - field).astype(jnp.bfloat16)

time: 256 us -> 268 us (1.047)
  waiting for transfers between devices: 146 us -> 178 us
  blocking collectives: 24.6 us -> 0 us
  other arithmetic: 47.6 us -> 51.1 us
    all_gather x0 -> x1, waiting for transfers between devices: none -> 31.8 us  [body(): summed = jnp.sum(lax.all_gather(partial_field, 'lag'), axis=0)]
    psum x1 -> x0, blocking collectives: 24.6 us -> none  [body(): summed = lax.psum(partial_field, 'lag')]
    reduce_sum x0 -> x1, other arithmetic: none -> 3.5 us  [body(): summed = jnp.sum(lax.all_gather(partial_field, 'lag'), axis=0)]
  transfers between devices with their start and end apart: 2 -> 3, of which waited for: 2 -> 3; matrix products, arithmetic and copies ran while one was open for 0% -> 0% of each run, Pallas kernels for 0% -> 0%
where the time goes in v1:
time: 268 us; the launch traced here: 267 us
  waiting for transfers between devices  178 us (66%)
  other arithmetic  51.1 us (19%)
  matrix products  15.7 us (6%)
  between operations  13.8 us (5%)
  local copies, waits for them, and re-layouts  8.12 us (3%)
    all_gather x1, waiting for transfers between devices, body(): gathered = lax.all_gather(hist16, 'grp', axis=1, tiled=True)  73.4 us
    reduce_scatter x1, waiting for transfers between devices, body(): mine = lax.psum_scatter(summed, 'grp', scatter_dimension=0, tiled=True)  72.6 us
    scatter-add x1, other arithmetic, body(): partial_field = jax.ops.segment_sum(terms, tile_obs, num_segments=observers)  44.7 us
    all_gather x1, waiting for transfers between devices, body(): summed = jnp.sum(lax.all_gather(partial_field, 'lag'), axis=0)  31.8 us
    dot_general x1, matrix products, body(): jnp.einsum('kas,kos->kao', picked, tiles, preferred_element_type=jnp.floa...  15 us
    gather x1, local copies, waits for them, and re-layouts, body(): picked = flat[tile_lag * source_count + tile_src]  6.55 us
  transfers between devices with their start and end apart: 3, of which 3 were waited for; matrix products, arithmetic and copies ran while one was open for 0% of the time, Pallas kernels for 0%

profile of v1, /device:TPU:0, one launch (start us, length us, event | category | flops | bytes accessed | tf_op | source)
XLA Modules:
  0.0 266.7 jit_solution(8765162983961375980)
XLA Ops:
  7.2 0.0 copy-start
  7.2 0.0 all-gather.4.cloned.1.call-start
  7.2 2.1 convert_element_type.6
  9.4 0.0 all-gather.4.cloned.1.call-update
  9.4 0.0 all-gather.6.cloned.1.call-start
  9.4 0.7 compare_select_fusion
  10.2 73.4 %all-gather.4.cloned.1.call-done = bf16[2,512,32,128]{3,2,1,0:T(8,128)(2,1)} async-done(((bf16[2,32,32,128]{3,2,1,0:T(8,128)(2,1)}), bf16[2,512,32,128]{3,2,1,0:T(8,128)(2,1)}) %all-gather.4.cloned.1.call-update) | async-done | bytes 8388624 | tf_op jit(solution)/shard_map/all_gather | solution.py:11
  83.6 6.5 %gather_fusion = bf16[512,32,128]{2,1,0:T(8,128)(2,1)} fusion(bf16[1024,32,128]{2,1,0:T(8,128)(2,1)} %bitcast.6, s32[1024]{0:T(1024)S(1)} %pad_clamp_fusion), kind=kCustom, calls=%fused_computation | custom fusion | bytes 8390656 | tf_op jit(solution)/shard_map/gather | solution.py:15
  90.1 0.0 copy-start.4
  90.1 15.0 %fusion.1 = f32[512,32,128]{2,1,0:T(8,128)} fusion(bf16[512,32,128]{2,1,0:T(8,128)(2,1)} %gather_fusion, bf16[512,128,128]{2,1,0:T(8,128)(2,1)} %param.8), kind=kOutput, calls=%fused_computation.7 | convolution fusion | flops 536870912 | bytes 29360128 | tf_op jit(solution)/shard_map/kas,kos->kao/dot_general | solution.py:16
  105.2 0.0 copy-done.4
  105.2 0.0 copy-start.3
  105.2 44.7 %scatter_fusion = f32[32,32,128]{2,1,0:T(8,128)S(1)} fusion(f32[32,32,128]{2,1,0:T(8,128)S(1)} %broadcast_in_dim.9, s32[512]{0:T(512)S(1)} %copy-done.4, f32[512,32,128]{2,1,0:T(8,128)} %fusion.1), kind=kCustom, calls=%fused_computation.1 | custom fusion | flops 2097152 | bytes 25167872 | tf_op jit(solution)/shard_map/scatter-add | solution.py:18
  149.9 0.0 copy-start.1
  149.9 0.8 copy-done.1
  150.7 0.0 all-gather.6.cloned.1.call-update
  150.7 0.0 reduce-scatter.2.cloned.1.call-start
  150.8 31.8 %all-gather.6.cloned.1.call-done = f32[256,32,128]{2,1,0:T(8,128)} async-done(((f32[32,32,128]{2,1,0:T(8,128)}), f32[256,32,128]{2,1,0:T(8,128)}) %all-gather.6.cloned.1.call-update) | async-done | bytes 4194320 | tf_op jit(solution)/shard_map/all_gather | solution.py:20
  182.6 3.5 %reduce_sum.9 = f32[32,32,128]{2,1,0:T(8,128)} reduce(f32[8,32,32,128]{3,2,1,0:T(8,128)} %bitcast.5, f32[]{:T(128)} %constant.7.clone.1), dimensions={0}, to_apply=%region_1.0 | reduce | flops 917504 | bytes 4718596 | tf_op jit(solution)/shard_map/reduce_sum | solution.py:20
  186.1 0.0 reduce-scatter.2.cloned.1.call-update
  186.1 72.6 %reduce-scatter.2.cloned.1.call-done = f32[2,32,128]{2,1,0:T(8,128)} async-done(((f32[32,32,128]{2,1,0:T(8,128)}), f32[2,32,128]{2,1,0:T(8,128)}) %reduce-scatter.2.cloned.1.call-update) | async-done | bytes 32784 | tf_op jit(solution)/shard_map/reduce_scatter | solution.py:21
  258.7 0.7 constant_dynamic-slice_fusion
  259.4 0.0 copy-done
  259.4 0.0 copy-done.3
  259.4 0.0 copy-start.2
  259.4 0.7 fusion
  260.1 0.0 copy-done.2
  (2 shorter events, 0.1 us)
Async XLA Ops:
  7.2 252.2 %copy-start = (bf16[2,128,128]{2,1,0:T(8,128)(2,1)S(1)}, bf16[2,128,128]{2,1,0:T(8,128)(2,1)}, u32[]{:S(2)}) copy-start(bf16[2,128,128]{2,1,0:T(8,128)(2,1)} %param.13) | copy-start | bytes 196612
  7.2 76.4 %all-gather.4.cloned.1.call-start = ((), (), s32[]{:S(2)}) async-start(), calls=%async_computation.1 | async-start | bytes 8912896 | tf_op jit(solution)/shard_map/all_gather | solution.py:11
  9.4 173.2 %all-gather.6.cloned.1.call-start = ((), (), s32[]{:S(2)}) async-start(), calls=%async_computation.3 | async-start | bytes 4718592 | tf_op jit(solution)/shard_map/all_gather | solution.py:20
  90.1 15.0 %copy-start.4 = (s32[512]{0:T(512)S(1)}, s32[512]{0:T(512)}, u32[]{:S(2)}) copy-start(s32[512]{0:T(512)} %param.10) | copy-start | bytes 6148
  105.2 154.2 %copy-start.3 = (f32[2,4,128]{2,1,0:T(4,128)S(1)}, f32[2,4,128]{2,1,0:T(4,128)}, u32[]{:S(2)}) copy-start(f32[2,4,128]{2,1,0:T(4,128)} %param.12) | copy-start | bytes 12292
  149.9 0.8 copy-start.1
  150.7 108.0 %reduce-scatter.2.cloned.1.call-start = ((), (), s32[]{:S(2)}) async-start(), calls=%async_computation.2 | async-start | bytes 557056 | tf_op jit(solution)/shard_map/reduce_scatter | solution.py:21
  259.4 0.7 copy-start.2
Sparse Core Ops, SparseCore 0:
  10.2 73.3 all-gather.3
  150.8 31.6 all-gather.5
  186.2 72.4 reduce-scatter.1
